TPU v7x, 512 devices: a whole 4x4x16 slice. The times are simulated.
512 devices in a mesh: dp: 4 (over z_hi, core), wide: 16 (over y, x), narrow: 8 (over z_lo).
Axes of the slice: x: 4, y: 4, z: 16 (z_hi: 2, z_lo: 8; z = z_hi * 8 + z_lo), core: 2. Of those that a mesh axis runs over, the one named last changes fastest.
Arguments:
- patches: bfloat16 [1024, 4, 6144], P('wide', 'dp'), parts along dimension 1, may hold values from -6 to 6
- vit_gain: float32 [6144], replicated, may hold values from 0.1 to 1.9
- vit_qkv: bfloat16 [6144, 3, 32, 128], P('narrow', None, 'wide'), may hold values from -4 to 4
- vit_in: bfloat16 [6144, 12288], P('narrow', 'wide'), may hold values from -0.078125 to 0.078125
- vit_attn_out: bfloat16 [4096, 6144], P('wide', 'narrow'), may hold values from -1 to 1
- vit_mlp_out: bfloat16 [12288, 6144], P('wide', 'narrow'), may hold values from -0.109375 to 0.109375
- proj: bfloat16 [6144, 4096], P('narrow', 'wide'), may hold values from -0.01953125 to 0.01953125
Outputs:
- encoded: bfloat16 [1024, 4, 4096], P('wide', 'dp', 'narrow'), parts along dimension 1
There are 4 independent parts, one for each index of `dp`. A program takes and returns all parts, laid end to end along the dimension named above; an argument that names none is the same for every part. Nothing has to cross between parts.
All inputs are finite; a program needn't handle non-finite values.
Results may differ from a plain program's by a relative error of at most 0.035.
Values may be sent and summed in bfloat16 or wider, within the bound.
No kernel may reach another device: no remote copies, remote signals or barrier semaphores. Data moves between devices by JAX's collectives and lax.ppermute only.
A program may use at most 64 MiB of HBM per device.

v0:
```python
import math
import jax
import jax.numpy as jnp
from jax import lax
from jax.sharding import PartitionSpec as P


def layer_norm(inputs, gain_row):
    widened = inputs.astype(jnp.float32)
    centred = widened - jnp.mean(widened, axis=-1, keepdims=True)
    variance = jnp.mean(centred * centred, axis=-1, keepdims=True)
    return (centred * lax.rsqrt(variance + 1e-06) * gain_row).astype(jnp.bfloat16)


def attend(queries, keys_all, values_all):
    score_scale = 1.0 / math.sqrt(queries.shape[-1])
    scores = (
        jnp.einsum("pihd,qihd->ihpq", queries, keys_all, preferred_element_type=jnp.float32)
        * score_scale
    )
    highest = jnp.max(scores, axis=-1, keepdims=True)
    exponentials = jnp.exp(scores - highest)
    totals = jnp.sum(exponentials, axis=-1)
    weights = exponentials.astype(jnp.bfloat16)
    mixed_sum = jnp.einsum(
        "ihpq,qihd->pihd", weights, values_all, preferred_element_type=jnp.float32
    )
    return (mixed_sum / jnp.transpose(totals, (2, 0, 1))[..., None]).astype(jnp.bfloat16)


def per_device(patches, vit_gain, vit_qkv, vit_in, vit_attn_out, vit_mlp_out, proj):
    local_rows = patches.shape[0]
    images = patches.shape[1]
    feature_block = vit_in.shape[0]
    heads_here = vit_qkv.shape[2]
    head_width = vit_qkv.shape[3]
    qkv_cols = 3 * heads_here * head_width
    narrow_start = lax.axis_index("narrow") * feature_block
    normed = layer_norm(patches, vit_gain)
    normed_part = lax.dynamic_slice_in_dim(normed, narrow_start, feature_block, 2)
    in_weight = jnp.concatenate([vit_qkv.reshape(feature_block, qkv_cols), vit_in], axis=1)
    piece_rows = lax.all_gather(normed_part, "wide", axis=0, tiled=True)
    flat_rows = piece_rows.reshape(-1, feature_block)
    joined = jnp.dot(flat_rows, in_weight, preferred_element_type=jnp.float32)
    partial_in = joined.reshape(piece_rows.shape[0], images, -1)
    summed_in = lax.psum(partial_in.astype(jnp.bfloat16), "narrow").astype(jnp.float32)
    row_count = summed_in.shape[0]
    qkv_all = (
        summed_in[..., :qkv_cols]
        .astype(jnp.bfloat16)
        .reshape(row_count, images, 3, heads_here, head_width)
    )
    activated = jax.nn.gelu(summed_in[..., qkv_cols:], approximate=False).astype(jnp.bfloat16)
    qkv_all, act_rows = (qkv_all, activated)
    mixed_heads = attend(qkv_all[:, :, 0], qkv_all[:, :, 1], qkv_all[:, :, 2])
    mixed_rows = mixed_heads.reshape(mixed_heads.shape[0], images, heads_here * head_width)
    heads_rows = mixed_rows.reshape(lax.axis_size("wide") * local_rows * images, -1)
    units_rows = act_rows.reshape(lax.axis_size("wide") * local_rows * images, -1)
    branch_terms = jnp.dot(heads_rows, vit_attn_out, preferred_element_type=jnp.float32)
    branch_terms = branch_terms + jnp.dot(
        units_rows, vit_mlp_out, preferred_element_type=jnp.float32
    )
    branch_sum = lax.psum_scatter(
        branch_terms.reshape(lax.axis_size("wide") * local_rows, images, -1).astype(jnp.bfloat16),
        "wide",
        scatter_dimension=0,
        tiled=True,
    ).astype(jnp.float32)
    own_columns = lax.dynamic_slice_in_dim(patches, narrow_start, feature_block, 2)
    vit_output = (own_columns.astype(jnp.float32) + branch_sum).astype(jnp.bfloat16)
    flat_output = vit_output.reshape(local_rows * images, feature_block)
    partial_encoded = jnp.dot(
        flat_output,
        lax.all_gather(proj, "wide", axis=1, tiled=True),
        preferred_element_type=jnp.float32,
    ).reshape(local_rows, images, -1)
    encoded = lax.psum_scatter(
        partial_encoded.astype(jnp.bfloat16), "narrow", scatter_dimension=2, tiled=True
    )
    return encoded


def solution(mesh):
    return jax.shard_map(
        per_device,
        mesh=mesh,
        in_specs=(
            P("wide", "dp", None),
            P(),
            P("narrow", None, "wide", None),
            P("narrow", "wide"),
            P("wide", "narrow"),
            P("wide", "narrow"),
            P("narrow", "wide"),
        ),
        out_specs=P("wide", "dp", "narrow"),
        check_vma=False,
    )
```

profile of v0, /device:TPU:4, one launch (start us, length us, event | category | flops | bytes accessed | tf_op | source)
XLA Modules:
  0.0 516.1 jit_solution(944441990527074840)
XLA Ops:
  6.5 0.0 copy-start
  6.5 0.0 all-gather.3.cloned.1.call-start
  6.5 1.4 convert_reduce_fusion
  8.0 1.5 multiply_reduce_fusion.1
  9.5 0.8 dynamic-slice
  10.3 0.7 fusion.86
  11.0 0.0 all-gather.3.cloned.1.call-update
  11.0 0.0 all-reduce.2.cloned.1.call-start
  11.1 3.1 reshape.76
  14.3 59.6 %all-gather.3.cloned.1.call-done = bf16[1024,1,768]{2,0,1:T(8,128)(2,1)} async-done(((bf16[64,1,768]{2,0,1:T(8,128)(2,1)}), bf16[1024,1,768]{2,0,1:T(8,128)(2,1)}) %all-gather.3.cloned.1.call-update) | async-done | bytes 1572880 | tf_op jit(solution)/shard_map/all_gather | solution.py:42
  73.9 6.0 %fusion.7 = bf16[1024,1,1536]{2,0,1:T(8,128)(2,1)} fusion(bf16[768,768]{1,0:T(8,128)(2,1)} %param.10, bf16[768,768]{1,0:T(8,128)(2,1)S(1)} %reshape.76, bf16[1024,1,768]{2,0,1:T(8,128)(2,1)} %all-gather.3.cloned.1.call-done), kind=kOutput, calls=%fused_computation.13 | convolution fusion | flops 2422210560 | bytes 7077888 | tf_op jit(solution)/shard_map/dot_general | solution.py:44
  79.9 0.0 all-reduce.2.cloned.1.call-update
  79.9 0.0 reduce-scatter.3.cloned.1.call-start
  80.0 166.4 %all-reduce.2.cloned.1.call-done = bf16[1024,1,1536]{2,0,1:T(8,128)(2,1)} async-done(((bf16[1024,1,1536]{2,0,1:T(8,128)(2,1)}), bf16[1024,1,1536]{2,0,1:T(8,128)(2,1)}) %all-reduce.2.cloned.1.call-update) | async-done | bytes 3145744 | tf_op jit(solution)/shard_map/psum | solution.py:46
  246.4 2.7 slice.25
  249.0 3.3 reshape.77
  252.4 2.1 fusion.123
  254.4 0.6 copy.13
  255.0 2.5 multiply_reduce_fusion
  257.5 1.4 fusion
  258.9 0.0 copy-start.1
  258.9 1.7 divide_convert_fusion
  260.6 0.0 copy-done
  260.6 0.2 copy-done.1
  260.8 0.0 copy-start.2
  260.8 7.8 %fusion.43 = f32[1024,768]{1,0:T(8,128)S(1)} fusion(bf16[768,768]{1,0:T(8,128)(2,1)S(1)} %copy-done, bf16[1024,1,1536]{2,0,1:T(8,128)(2,1)S(1)} %copy-done.1), kind=kOutput, calls=%fused_computation.52 | convolution fusion | flops 1259864064 | bytes 5898240 | tf_op jit(solution)/shard_map/dot_general | solution.py:60
  268.6 0.0 copy-done.2
  268.6 1.8 fusion.77
  270.4 0.0 reduce-scatter.3.cloned.1.call-update
  270.4 0.0 all-gather.5.cloned.1.call-start
  270.5 0.5 all-gather.5.cloned.1.call-update
  271.0 0.0 reduce-scatter.5.cloned.1.call-start
  271.1 84.1 %reduce-scatter.3.cloned.1.call-done = bf16[64,1,768]{2,0,1:T(8,128)(2,1)} async-done(((bf16[1024,1,768]{2,0,1:T(8,128)(2,1)}), bf16[64,1,768]{2,0,1:T(8,128)(2,1)}) %reduce-scatter.3.cloned.1.call-update) | async-done | bytes 98320 | tf_op jit(solution)/shard_map/reduce_scatter | solution.py:63
  355.1 83.4 %all-gather.5.cloned.1.call-done = bf16[768,4096]{1,0:T(8,128)(2,1)} async-done(((bf16[768,256]{1,0:T(8,128)(2,1)}), bf16[768,4096]{1,0:T(8,128)(2,1)}) %all-gather.5.cloned.1.call-update) | async-done | bytes 6291472 | tf_op jit(solution)/shard_map/all_gather | solution.py:74
  438.5 4.9 fusion.2
  443.4 0.0 reduce-scatter.5.cloned.1.call-update
  443.4 66.2 %reduce-scatter.5.cloned.1.call-done = bf16[64,1,512]{2,0,1:T(8,128)(2,1)} async-done(((bf16[64,1,4096]{2,0,1:T(8,128)(2,1)}), bf16[64,1,512]{2,0,1:T(8,128)(2,1)}) %reduce-scatter.5.cloned.1.call-update) | async-done | bytes 65552 | tf_op jit(solution)/shard_map/reduce_scatter | solution.py:77
  (2 shorter events, 0.0 us)
Async XLA Ops:
  6.5 254.0 %copy-start = (bf16[768,768]{1,0:T(8,128)(2,1)S(1)}, bf16[768,768]{1,0:T(8,128)(2,1)}, u32[]{:S(2)}) copy-start(bf16[768,768]{1,0:T(8,128)(2,1)} %param.12) | copy-start | bytes 3538948
  6.5 67.3 %all-gather.3.cloned.1.call-start = ((), (), s32[]{:S(2)}) async-start(), calls=%async_computation.2 | async-start | bytes 1671168 | tf_op jit(solution)/shard_map/all_gather | solution.py:42
  11.0 235.3 %all-reduce.2.cloned.1.call-start = ((), (), s32[]{:S(2)}) async-start(), calls=%async_computation.3 | async-start | bytes 6291456 | tf_op jit(solution)/shard_map/psum | solution.py:46
  79.9 275.2 %reduce-scatter.3.cloned.1.call-start = ((), (), s32[]{:S(2)}) async-start(), calls=%async_computation.4 | async-start | bytes 1671168 | tf_op jit(solution)/shard_map/reduce_scatter | solution.py:63
  258.9 1.9 copy-start.1
  260.8 7.8 %copy-start.2 = (bf16[256,768]{1,0:T(8,128)(2,1)S(1)}, bf16[256,768]{1,0:T(8,128)(2,1)}, u32[]{:S(2)}) copy-start(bf16[256,768]{1,0:T(8,128)(2,1)} %param.11) | copy-start | bytes 1179652
  270.4 168.0 %all-gather.5.cloned.1.call-start = ((), (), s32[]{:S(2)}) async-start(), calls=%async_computation.5 | async-start | bytes 6684672 | tf_op jit(solution)/shard_map/all_gather | solution.py:74
  271.0 238.6 %reduce-scatter.5.cloned.1.call-start = ((), (), s32[]{:S(2)}) async-start(), calls=%async_computation.6 | async-start | bytes 589824 | tf_op jit(solution)/shard_map/reduce_scatter | solution.py:77
Sparse Core Ops, SparseCore 0:
  11.2 62.6 all-gather.2
  80.0 166.2 all-reduce.1
  270.5 84.5 reduce-scatter.2
  358.0 80.4 all-gather.4
  443.5 66.0 reduce-scatter.4
where the time goes:
time: 517 us; the launch traced here: 516 us
  waiting for transfers between devices  460 us (89%)
  matrix products  24.7 us (5%)
  between operations  13.2 us (3%)
  local copies, waits for them, and re-layouts  12.8 us (2%)
    psum x1, waiting for transfers between devices, per_device(): lax.psum(partial_in.astype(jnp.bfloat16), 'narrow').astype(jnp.float32)  166 us
    reduce_scatter x1, waiting for transfers between devices, per_device(): lax.psum_scatter(branch_terms.reshape(lax.axis_size('wide') * local_rows,...  84.1 us
    all_gather x1, waiting for transfers between devices, per_device(): lax.all_gather(proj, 'wide', axis=1, tiled=True)  83.4 us
    reduce_scatter x1, waiting for transfers between devices, per_device(): lax.psum_scatter(partial_encoded.astype(jnp.bfloat16), 'narrow', scatter_...  66.2 us
    all_gather x1, waiting for transfers between devices, per_device(): piece_rows = lax.all_gather(normed_part, 'wide', axis=0, tiled=True)  59.6 us
  transfers between devices with their start and end apart: 5, of which 5 were waited for; matrix products, arithmetic and copies ran while one was open for 1% of the time, Pallas kernels for 0%

commit v1 on v0

--- a/solution.py
+++ b/solution.py
@@ -3,6 +3,14 @@
 import jax.numpy as jnp
 from jax import lax
 from jax.sharding import PartitionSpec as P
+
+
+def _note_cells(frame):
+    answer = lax.axis_size("wide")
+    local_next = jnp.stack(answer * [frame], axis=0)
+    earlier = lax.all_to_all(local_next, "wide", 0, 0)
+    step_out = jnp.concatenate(earlier, axis=1)
+    return step_out
 
 
 def layer_norm(inputs, gain_row):
@@ -70,9 +78,7 @@
     vit_output = (own_columns.astype(jnp.float32) + branch_sum).astype(jnp.bfloat16)
     flat_output = vit_output.reshape(local_rows * images, feature_block)
     partial_encoded = jnp.dot(
-        flat_output,
-        lax.all_gather(proj, "wide", axis=1, tiled=True),
-        preferred_element_type=jnp.float32,
+        flat_output, _note_cells(proj), preferred_element_type=jnp.float32
     ).reshape(local_rows, images, -1)
     encoded = lax.psum_scatter(
         partial_encoded.astype(jnp.bfloat16), "narrow", scatter_dimension=2, tiled=True

time: 517 us -> 433 us (0.84)
  waiting for transfers between devices: 460 us -> 365 us
  starting transfers between devices: 0.17 us -> 6.3 us
    all_gather x1 -> x0, waiting for transfers between devices: 83.4 us -> none  [per_device(): lax.all_gather(proj, 'wide', axis=1, tiled=True)]
    psum x1, waiting for transfers between devices: 166 us -> 156 us  [per_device(): lax.psum(partial_in.astype(jnp.bfloat16), 'narrow').astype(jnp.float32)]
    all_to_all x0 -> x1, starting transfers between devices: none -> 6.18 us  [_note_cells(): earlier = lax.all_to_all(local_next, 'wide', 0, 0)]
  transfers between devices with their start and end apart: 5 -> 5, of which waited for: 5 -> 4; matrix products, arithmetic and copies ran while one was open for 1% -> 7% of each run, Pallas kernels for 0% -> 0%
where the time goes in v1:
time: 433 us; the launch traced here: 432 us
  waiting for transfers between devices  365 us (84%)
  matrix products  25.5 us (6%)
  local copies, waits for them, and re-layouts  17.2 us (4%)
  between operations  13.2 us (3%)
  starting transfers between devices  6.3 us (1%)
  other arithmetic  5.06 us (1%)
    psum x1, waiting for transfers between devices, per_device(): lax.psum(partial_in.astype(jnp.bfloat16), 'narrow').astype(jnp.float32)  156 us
    reduce_scatter x1, waiting for transfers between devices, per_device(): lax.psum_scatter(branch_terms.reshape(lax.axis_size('wide') * local_rows,...  84.6 us
    reduce_scatter x1, waiting for transfers between devices, per_device(): lax.psum_scatter(partial_encoded.astype(jnp.bfloat16), 'narrow', scatter_...  65 us
    all_gather x1, waiting for transfers between devices, per_device(): piece_rows = lax.all_gather(normed_part, 'wide', axis=0, tiled=True)  59.6 us
  transfers between devices with their start and end apart: 5, of which 4 were waited for; matrix products, arithmetic and copies ran while one was open for 7% of the time, Pallas kernels for 0%

profile of v1, /device:TPU:4, one launch (start us, length us, event | category | flops | bytes accessed | tf_op | source)
XLA Modules:
  0.0 432.3 jit_solution(6975898468878738226)
XLA Ops:
  6.5 0.0 copy-start
  6.5 0.0 all-gather.2.cloned.1.call-start
  6.5 1.4 convert_reduce_fusion
  8.0 1.5 multiply_reduce_fusion.1
  9.5 0.8 dynamic-slice
  10.3 0.7 fusion.86
  11.0 0.0 all-gather.2.cloned.1.call-update
  11.0 0.0 all-reduce.2.cloned.1.call-start
  11.1 3.1 reshape.84
  14.3 59.6 %all-gather.2.cloned.1.call-done = bf16[1024,1,768]{2,0,1:T(8,128)(2,1)} async-done(((bf16[64,1,768]{2,0,1:T(8,128)(2,1)}), bf16[1024,1,768]{2,0,1:T(8,128)(2,1)}) %all-gather.2.cloned.1.call-update) | async-done | bytes 1572880 | tf_op jit(solution)/shard_map/all_gather | solution.py:50
  73.9 6.0 %fusion.7 = bf16[1024,1,1536]{2,0,1:T(8,128)(2,1)} fusion(bf16[768,768]{1,0:T(8,128)(2,1)} %param.10, bf16[768,768]{1,0:T(8,128)(2,1)S(1)} %reshape.84, bf16[1024,1,768]{2,0,1:T(8,128)(2,1)} %all-gather.2.cloned.1.call-done), kind=kOutput, calls=%fused_computation.13 | convolution fusion | flops 2422210560 | bytes 7077888 | tf_op jit(solution)/shard_map/dot_general | solution.py:52
  79.9 0.0 copy-start.2
  79.9 0.0 all-reduce.2.cloned.1.call-update
  79.9 1.0 copy-done.2
  80.9 0.2 copy.16
  81.0 3.3 stack.2
  84.3 6.2 %all-to-all-start = ((bf16[16,768,256]{1,2,0:T(8,128)(2,1)}), bf16[16,768,256]{1,2,0:T(8,128)(2,1)}, u32[]{:S(2)}, u32[]{:S(2)}) async-start(bf16[16,768,256]{1,2,0:T(8,128)(2,1)} %stack.2), calls=%async_computation.1 | async-start | bytes 12582912 | tf_op jit(solution)/shard_map/all_to_all | solution.py:11
  90.5 0.0 reduce-scatter.3.cloned.1.call-start
  90.5 155.8 %all-reduce.2.cloned.1.call-done = bf16[1024,1,1536]{2,0,1:T(8,128)(2,1)} async-done(((bf16[1024,1,1536]{2,0,1:T(8,128)(2,1)}), bf16[1024,1,1536]{2,0,1:T(8,128)(2,1)}) %all-reduce.2.cloned.1.call-update) | async-done | bytes 3145744 | tf_op jit(solution)/shard_map/psum | solution.py:54
  246.3 2.7 slice.25
  249.0 3.3 reshape.85
  252.3 2.1 fusion.123
  254.4 0.6 copy.18
  255.0 2.5 multiply_reduce_fusion
  257.5 1.4 fusion
  258.8 0.0 copy-start.1
  258.9 1.7 divide_convert_fusion
  260.5 0.0 copy-done
  260.5 0.2 copy-done.1
  260.7 0.0 copy-start.3
  260.7 7.8 %fusion.43 = f32[1024,768]{1,0:T(8,128)S(1)} fusion(bf16[768,768]{1,0:T(8,128)(2,1)S(1)} %copy-done, bf16[1024,1,1536]{2,0,1:T(8,128)(2,1)S(1)} %copy-done.1), kind=kOutput, calls=%fused_computation.52 | convolution fusion | flops 1259864064 | bytes 5898240 | tf_op jit(solution)/shard_map/dot_general | solution.py:68
  268.6 0.0 copy-done.3
  268.6 1.8 fusion.77
  270.4 0.0 reduce-scatter.3.cloned.1.call-update
  270.4 0.0 reduce-scatter.5.cloned.1.call-start
  270.5 0.0 all-to-all-done
  270.5 84.6 %reduce-scatter.3.cloned.1.call-done = bf16[64,1,768]{2,0,1:T(8,128)(2,1)} async-done(((bf16[1024,1,768]{2,0,1:T(8,128)(2,1)}), bf16[64,1,768]{2,0,1:T(8,128)(2,1)}) %reduce-scatter.3.cloned.1.call-update) | async-done | bytes 98320 | tf_op jit(solution)/shard_map/reduce_scatter | solution.py:71
  355.1 5.7 %fusion.2 = bf16[64,1,4096]{2,0,1:T(8,128)(2,1)} fusion(bf16[768,4096]{0,1:T(8,128)(2,1)} %bitcast.15, bf16[64,1,768]{2,0,1:T(8,128)(2,1)} %reduce-scatter.3.cloned.1.call-done, bf16[64,1,6144]{2,0,1:T(8,128)(2,1)} %param.7, s32[]{:T(128)S(6)} %select_n.4), kind=kOutput, calls=%fused_computation.6 | convolution fusion | flops 403111936 | bytes 7012356 | tf_op jit(solution)/shard_map/dot_general | solution.py:80
  360.8 0.0 reduce-scatter.5.cloned.1.call-update
  360.8 65.0 %reduce-scatter.5.cloned.1.call-done = bf16[64,1,512]{2,0,1:T(8,128)(2,1)} async-done(((bf16[64,1,4096]{2,0,1:T(8,128)(2,1)}), bf16[64,1,512]{2,0,1:T(8,128)(2,1)}) %reduce-scatter.5.cloned.1.call-update) | async-done | bytes 65552 | tf_op jit(solution)/shard_map/reduce_scatter | solution.py:83
  (2 shorter events, 0.0 us)
Async XLA Ops:
  6.5 254.0 %copy-start = (bf16[768,768]{1,0:T(8,128)(2,1)S(1)}, bf16[768,768]{1,0:T(8,128)(2,1)}, u32[]{:S(2)}) copy-start(bf16[768,768]{1,0:T(8,128)(2,1)} %param.12) | copy-start | bytes 3538948
  6.5 67.3 %all-gather.2.cloned.1.call-start = ((), (), s32[]{:S(2)}) async-start(), calls=%async_computation.3 | async-start | bytes 1671168 | tf_op jit(solution)/shard_map/all_gather | solution.py:50
  11.0 235.3 %all-reduce.2.cloned.1.call-start = ((), (), s32[]{:S(2)}) async-start(), calls=%async_computation.4 | async-start | bytes 6291456 | tf_op jit(solution)/shard_map/psum | solution.py:54
  79.9 1.0 copy-start.2
  84.3 186.2 %all-to-all-start = ((bf16[16,768,256]{1,2,0:T(8,128)(2,1)}), bf16[16,768,256]{1,2,0:T(8,128)(2,1)}, u32[]{:S(2)}, u32[]{:S(2)}) async-start(bf16[16,768,256]{1,2,0:T(8,128)(2,1)} %stack.2), calls=%async_computation.1 | async-start | bytes 12582912 | tf_op jit(solution)/shard_map/all_to_all | solution.py:11
  90.5 264.6 %reduce-scatter.3.cloned.1.call-start = ((), (), s32[]{:S(2)}) async-start(), calls=%async_computation.5 | async-start | bytes 1671168 | tf_op jit(solution)/shard_map/reduce_scatter | solution.py:71
  258.8 1.9 copy-start.1
  260.7 7.8 %copy-start.3 = (bf16[256,768]{1,0:T(8,128)(2,1)S(1)}, bf16[256,768]{1,0:T(8,128)(2,1)}, u32[]{:S(2)}) copy-start(bf16[256,768]{1,0:T(8,128)(2,1)} %param.11) | copy-start | bytes 1179652
  270.4 155.3 %reduce-scatter.5.cloned.1.call-start = ((), (), s32[]{:S(2)}) async-start(), calls=%async_computation.6 | async-start | bytes 589824 | tf_op jit(solution)/shard_map/reduce_scatter | solution.py:83
Sparse Core Ops, SparseCore 0:
  11.2 62.6 all-gather.1
  80.0 166.2 all-reduce.1
  270.6 84.4 reduce-scatter.2
  360.9 64.8 reduce-scatter.4

commit v2 on v0

--- a/solution.py
+++ b/solution.py
@@ -3,6 +3,11 @@
 import jax.numpy as jnp
 from jax import lax
 from jax.sharding import PartitionSpec as P
+
+
+def summed_here(x, axis):
+    parts = lax.all_gather(x, axis)
+    return jnp.sum(parts, axis=0)
 
 
 def layer_norm(inputs, gain_row):
@@ -43,7 +48,7 @@
     flat_rows = piece_rows.reshape(-1, feature_block)
     joined = jnp.dot(flat_rows, in_weight, preferred_element_type=jnp.float32)
     partial_in = joined.reshape(piece_rows.shape[0], images, -1)
-    summed_in = lax.psum(partial_in.astype(jnp.bfloat16), "narrow").astype(jnp.float32)
+    summed_in = summed_here(partial_in.astype(jnp.bfloat16), "narrow").astype(jnp.float32)
     row_count = summed_in.shape[0]
     qkv_all = (
         summed_in[..., :qkv_cols]

time: 517 us -> 827 us (1.60)
  waiting for transfers between devices: 460 us -> 760 us
  other arithmetic: 5.06 us -> 20.5 us
    all_gather x0 -> x1, waiting for transfers between devices: none -> 491 us  [summed_here(): parts = lax.all_gather(x, axis)]
    psum x1 -> x0, waiting for transfers between devices: 166 us -> none  [per_device(): lax.psum(partial_in.astype(jnp.bfloat16), 'narrow').astype(jnp.float32)]
    all_gather x1, waiting for transfers between devices: 83.4 us -> 49.8 us  [per_device(): lax.all_gather(proj, 'wide', axis=1, tiled=True)]
    reduce_sum x0 -> x1, other arithmetic: none -> 15.4 us  [summed_here(): return jnp.sum(parts, axis=0)]
    reduce_scatter x1, waiting for transfers between devices: 84.1 us -> 94.5 us  [per_device(): lax.psum_scatter(branch_terms.reshape(lax.axis_size('wide') * local_rows,...]
  transfers between devices with their start and end apart: 5 -> 5, of which waited for: 5 -> 5; matrix products, arithmetic and copies ran while one was open for 1% -> 5% of each run, Pallas kernels for 0% -> 0%
where the time goes in v2:
time: 827 us
  waiting for transfers between devices  760 us (92%)
  matrix products  25.9 us (3%)
  other arithmetic  20.5 us (2%)
  between operations  13.2 us (2%)
    all_gather x1, waiting for transfers between devices, summed_here(): parts = lax.all_gather(x, axis)  491 us
    reduce_scatter x1, waiting for transfers between devices, per_device(): lax.psum_scatter(branch_terms.reshape(lax.axis_size('wide') * local_rows,...  94.5 us
    reduce_scatter x1, waiting for transfers between devices, per_device(): lax.psum_scatter(partial_encoded.astype(jnp.bfloat16), 'narrow', scatter_...  65 us
    all_gather x1, waiting for transfers between devices, per_device(): piece_rows = lax.all_gather(normed_part, 'wide', axis=0, tiled=True)  59.6 us
    all_gather x1, waiting for transfers between devices, per_device(): lax.all_gather(proj, 'wide', axis=1, tiled=True)  49.8 us
  transfers between devices with their start and end apart: 5, of which 5 were waited for; matrix products, arithmetic and copies ran while one was open for 5% of the time, Pallas kernels for 0%

profile of v2, /device:TPU:4, one launch (start us, length us, event | category | flops | bytes accessed | tf_op | source)
XLA Modules:
  0.0 827.1 jit_solution(14936712825952552760)
XLA Ops:
  6.5 0.0 copy-start
  6.5 0.0 all-gather.5.cloned.1.call-start
  6.5 1.4 convert_reduce_fusion
  8.0 1.5 multiply_reduce_fusion.1
  9.5 0.8 dynamic-slice
  10.3 0.7 fusion.84
  11.0 0.0 all-gather.5.cloned.1.call-update
  11.0 0.0 all-gather.9.cloned.1.call-start
  11.1 3.1 reshape.88
  14.2 59.6 %all-gather.5.cloned.1.call-done = bf16[1024,1,768]{2,0,1:T(8,128)(2,1)} async-done(((bf16[64,1,768]{2,0,1:T(8,128)(2,1)}), bf16[1024,1,768]{2,0,1:T(8,128)(2,1)}) %all-gather.5.cloned.1.call-update) | async-done | bytes 1572880 | tf_op jit(solution)/shard_map/all_gather | solution.py:47
  73.8 6.0 convolution_convert_fusion.1
  79.8 0.0 all-gather.9.cloned.1.call-update
  79.8 0.0 all-gather.7.cloned.1.call-start
  79.9 0.7 all-gather.7.cloned.1.call-update
  80.6 0.0 reduce-scatter.3.cloned.1.call-start
  80.6 490.6 %all-gather.9.cloned.1.call-done = bf16[8192,1536]{1,0:T(8,128)(2,1)} async-done(((bf16[1024,1536]{1,0:T(8,128)(2,1)}), bf16[8192,1536]{1,0:T(8,128)(2,1)}) %all-gather.9.cloned.1.call-update) | async-done | bytes 25165840 | tf_op jit(solution)/shard_map/all_gather | solution.py:9
  571.2 15.4 %reduce.8 = bf16[1024,1536]{1,0:T(8,128)(2,1)} reduce(bf16[8,1024,1536]{2,1,0:T(8,128)(2,1)} %bitcast.47, bf16[]{:T(256)} %constant.10.clone.1), dimensions={0}, to_apply=%region_2.0 | reduce | flops 11010048 | bytes 28311554 | tf_op jit(solution)/shard_map/reduce_sum | solution.py:10
  586.7 1.5 slice.25
  588.2 1.7 copy.13
  589.8 2.5 multiply_reduce_fusion
  592.3 1.4 fusion
  593.7 0.0 copy-start.1
  593.7 2.9 divide_convert_fusion
  596.6 0.0 copy-done
  596.6 0.0 copy-done.1
  596.6 0.0 copy-start.2
  596.7 7.8 fusion.42
  604.5 0.0 copy-done.2
  604.5 1.8 fusion.76
  606.3 0.0 reduce-scatter.3.cloned.1.call-update
  606.3 0.0 reduce-scatter.5.cloned.1.call-start
  606.4 49.8 %all-gather.7.cloned.1.call-done = bf16[768,4096]{1,0:T(8,128)(2,1)} async-done(((bf16[768,256]{1,0:T(8,128)(2,1)}), bf16[768,4096]{1,0:T(8,128)(2,1)}) %all-gather.7.cloned.1.call-update) | async-done | bytes 6291472 | tf_op jit(solution)/shard_map/all_gather | solution.py:79
  656.1 94.5 %reduce-scatter.3.cloned.1.call-done = bf16[64,1,768]{2,0,1:T(8,128)(2,1)} async-done(((bf16[1024,1,768]{2,0,1:T(8,128)(2,1)}), bf16[64,1,768]{2,0,1:T(8,128)(2,1)}) %reduce-scatter.3.cloned.1.call-update) | async-done | bytes 98320 | tf_op jit(solution)/shard_map/reduce_scatter | solution.py:68
  750.6 4.9 fusion.2
  755.5 0.0 reduce-scatter.5.cloned.1.call-update
  755.6 65.0 %reduce-scatter.5.cloned.1.call-done = bf16[64,1,512]{2,0,1:T(8,128)(2,1)} async-done(((bf16[64,1,4096]{2,0,1:T(8,128)(2,1)}), bf16[64,1,512]{2,0,1:T(8,128)(2,1)}) %reduce-scatter.5.cloned.1.call-update) | async-done | bytes 65552 | tf_op jit(solution)/shard_map/reduce_scatter | solution.py:82
  (2 shorter events, 0.0 us)
Async XLA Ops:
  6.5 590.1 %copy-start = (bf16[768,768]{1,0:T(8,128)(2,1)S(1)}, bf16[768,768]{1,0:T(8,128)(2,1)}, u32[]{:S(2)}) copy-start(bf16[768,768]{1,0:T(8,128)(2,1)} %param.12) | copy-start | bytes 3538948
  6.5 67.3 %all-gather.5.cloned.1.call-start = ((), (), s32[]{:S(2)}) async-start(), calls=%async_computation.2 | async-start | bytes 1671168 | tf_op jit(solution)/shard_map/all_gather | solution.py:47
  11.0 560.2 %all-gather.9.cloned.1.call-start = ((), (), s32[]{:S(2)}) async-start(), calls=%async_computation.6 | async-start | bytes 28311552 | tf_op jit(solution)/shard_map/all_gather | solution.py:9
  79.8 576.3 %all-gather.7.cloned.1.call-start = ((), (), s32[]{:S(2)}) async-start(), calls=%async_computation.4 | async-start | bytes 6684672 | tf_op jit(solution)/shard_map/all_gather | solution.py:79
  80.6 670.0 %reduce-scatter.3.cloned.1.call-start = ((), (), s32[]{:S(2)}) async-start(), calls=%async_computation.3 | async-start | bytes 1671168 | tf_op jit(solution)/shard_map/reduce_scatter | solution.py:68
  593.7 2.9 copy-start.1
  596.6 7.9 copy-start.2
  606.3 214.3 %reduce-scatter.5.cloned.1.call-start = ((), (), s32[]{:S(2)}) async-start(), calls=%async_computation.5 | async-start | bytes 589824 | tf_op jit(solution)/shard_map/reduce_scatter | solution.py:82
Sparse Core Ops, SparseCore 0:
  11.1 62.6 all-gather.4
  80.0 491.2 all-gather.8
  574.2 81.8 all-gather.6
  660.1 90.4 reduce-scatter.2
  755.7 64.8 reduce-scatter.4
